TPU v7x, 256 devices: a whole 4x4x8 slice. The times are simulated.
256 devices in a mesh: member: 8 (over x, y_hi), space: 32 (over y_lo, z, core).
Axes of the slice: x: 4, y: 4 (y_hi: 2, y_lo: 2; y = y_hi * 2 + y_lo), z: 8, core: 2. Of those that a mesh axis runs over, the one named last changes fastest.
Arguments:
- ensemble: bfloat16 [256, 48, 16384], P('member', None, 'space')
- inflation: float32 [256, 128], P('member'), may hold values from 0.5 to 2
- weights: bfloat16 [128, 256, 256], P('space')
- region_ids: int32 [16384], P('space'), may hold values from 0 to 127, as said below
- extinction: float32 [48], replicated, may hold values from 0.1 to 2
- obs_cols: int32 [4096], P('space'), may hold values from 0 to 16383, as said below
Outputs:
- analysis: bfloat16 [256, 48, 16384], P('member', None, 'space')
- obs_analysis: float32 [256, 4096], P('member', 'space')
Inputs may be any that keep to these rules, and one draw needn't show every extreme that they name: `region_ids`: region r belongs to index r // 4 of space. Each block of 512 columns held by one index of space holds exactly 16 columns of the regions of every index of space. `obs_cols`: each observation's column lies in the block of 512 columns held by the same index of space as the observation.
All inputs are finite; a program needn't handle non-finite values.
Results may differ from a plain program's by a relative error of at most 0.0047.
Values may be sent and summed in bfloat16 or wider, within the bound.
No kernel may reach another device: no remote copies, remote signals or barrier semaphores. Data moves between devices by JAX's collectives and lax.ppermute only.
A program may use at most 64 MiB of HBM per device.

v0:
```python
import jax
import jax.numpy as jnp
from jax import lax
from jax.sharding import PartitionSpec as P


def local(ensemble, inflation, weights, region_ids, extinction, obs_cols):
    n_space = lax.axis_size("space")
    n_member = lax.axis_size("member")
    local_members = ensemble.shape[0]
    tracers = ensemble.shape[1]
    columns = ensemble.shape[2]
    members = local_members * n_member
    reg_count = weights.shape[0]
    all_regions = inflation.shape[1]
    send_cols = columns // n_space
    slot_cols = send_cols // n_member
    own_cols = n_space * slot_cols
    owner = region_ids // reg_count
    owner_hot = (owner[:, None] == jnp.arange(n_space, dtype=jnp.int32)[None, :]).astype(jnp.int32)
    before = jnp.cumsum(owner_hot, axis=0) - owner_hot
    rank_in = jnp.sum(before * owner_hot, axis=1)
    position = owner * send_cols + rank_in
    ordering = (
        jnp.zeros((columns,), jnp.int32).at[position].set(jnp.arange(columns, dtype=jnp.int32))
    )
    labels_all = jnp.take(region_ids % reg_count, ordering).reshape(n_space, n_member, slot_cols)
    my_labels = lax.dynamic_index_in_dim(labels_all, lax.axis_index("member"), 1, keepdims=False)
    got_labels = lax.all_to_all(
        my_labels, "space", split_axis=0, concat_axis=0, tiled=True
    ).reshape(own_cols)
    summed = lax.psum(jnp.sum(ensemble, axis=0, dtype=jnp.float32), "member")
    mean = summed / members
    region_hot = (jnp.arange(all_regions, dtype=jnp.int32)[:, None] == region_ids[None, :]).astype(
        jnp.float32
    )
    factor = jnp.dot(inflation, region_hot, precision=lax.Precision.HIGHEST)
    outgoing = ((ensemble.astype(jnp.float32) - mean[None]) * factor[:, None, :]).astype(
        jnp.bfloat16
    )
    rows_major = jnp.transpose(outgoing, (2, 0, 1)).reshape(columns, local_members * tracers)
    payload = jnp.take(rows_major, ordering, axis=0).reshape(
        n_space, n_member, slot_cols, local_members * tracers
    )
    received = lax.all_to_all(
        lax.all_to_all(payload, "member", split_axis=1, concat_axis=3, tiled=True),
        "space",
        split_axis=0,
        concat_axis=0,
        tiled=True,
    )
    gathered = received.reshape(own_cols, members, tracers)
    accum = jnp.zeros((own_cols, members, tracers), jnp.float32)
    for region in range(reg_count):
        partial_prod = jnp.einsum(
            "jk,cjt->ckt", weights[region], gathered, preferred_element_type=jnp.float32
        )
        accum = accum + jnp.where((got_labels == region)[:, None, None], partial_prod, 0.0)
    increment = accum.astype(jnp.bfloat16)
    result_rows = increment
    result_rows = result_rows.reshape(n_space, 1, slot_cols, members * tracers)
    halfway = lax.all_to_all(result_rows, "space", split_axis=0, concat_axis=0, tiled=True)
    returned = lax.all_to_all(halfway, "member", split_axis=3, concat_axis=1, tiled=True)
    restored = jnp.take(returned.reshape(columns, local_members * tracers), position, axis=0)
    restored = jnp.transpose(restored.reshape(columns, local_members, tracers), (1, 2, 0))
    analysis = (mean[None] + restored.astype(jnp.float32)).astype(jnp.bfloat16)
    local_index = obs_cols - lax.axis_index("space") * columns
    picked = jnp.take(analysis, local_index, axis=2).astype(jnp.float32)
    obs_analysis = jnp.einsum("t,kto->ko", extinction, picked, precision=lax.Precision.HIGHEST)
    return (analysis, obs_analysis)


def solution(mesh):
    in_specs = (
        P("member", None, "space"),
        P("member", None),
        P("space", None, None),
        P("space"),
        P(),
        P("space"),
    )
    out_specs = (P("member", None, "space"), P("member", "space"))
    return jax.shard_map(local, mesh=mesh, in_specs=in_specs, out_specs=out_specs, check_vma=False)
```

profile of v0, /device:TPU:64, one launch (start us, length us, event | category | flops | bytes accessed | tf_op | source)
XLA Modules:
  0.0 389.3 jit_solution(15727001249137828852)
XLA Ops:
  7.2 7.2 %copy.60 = bf16[32,48,512]{1,0,2:T(8,128)(2,1)} copy(bf16[32,48,512]{2,1,0:T(8,128)(2,1)} %param.8) | data formatting | bytes 3145728 | tf_op args[0]
  14.5 4.8 %convert_reduce_fusion = f32[48,512]{0,1:T(8,128)} fusion(bf16[32,48,512]{1,0,2:T(8,128)(2,1)} %copy.60), kind=kLoop, calls=%fused_computation.6 | loop fusion | flops 1548288 | bytes 1671168 | tf_op jit(solution)/shard_map/reduce_sum | solution.py:32
  20.9 2.4 scatter_custom_fusion
  23.6 3.5 gather_fusion
  27.2 83.8 %all-reduce.2.cloned.1.call-done = f32[48,512]{0,1:T(8,128)} async-done(((f32[48,512]{0,1:T(8,128)}), f32[48,512]{0,1:T(8,128)}) %all-reduce.2.cloned.1.call-update) | async-done | bytes 98320 | tf_op jit(solution)/shard_map/psum | solution.py:32
  112.0 5.8 %fusion.3 = bf16[512,32,48]{2,1,0:T(8,128)(2,1)} fusion(bf16[32,48,512]{1,0,2:T(8,128)(2,1)} %copy.60, f32[32,512]{0,1:T(8,128)S(1)} %copy.62, f32[48,512]{0,1:T(8,128)S(1)} %broadcast_multiply_fusion), kind=kLoop, calls=%fused_computation.11 | loop fusion | flops 3145728 | bytes 3309568 | tf_op jit(solution)/shard_map/transpose | solution.py:41
  117.8 4.4 %copy.63 = bf16[512,32,48]{0,2,1:T(8,128)(2,1)S(1)} copy(bf16[512,32,48]{2,1,0:T(8,128)(2,1)} %fusion.3) | data formatting | bytes 3145728 | tf_op jit(solution)/shard_map/transpose | solution.py:41
  123.0 2.9 gather_fusion.2
  128.2 2.4 copy.65
  130.6 3.6 all-to-all-start.1
  134.9 16.7 %all-to-all-done.1 = bf16[32,8,2,1536]{3,2,0,1:T(2,128)(2,1)S(1)} async-done(((bf16[32,8,2,1536]{3,2,0,1:T(2,128)(2,1)}), bf16[32,8,2,1536]{3,2,0,1:T(2,128)(2,1)S(1)}, u32[]{:S(2)}, u32[]{:S(2)}) %all-to-all-start.1) | async-done | bytes 1572896 | tf_op jit(solution)/shard_map/all_to_all | solution.py:46
  151.6 8.0 %all-to-all-start = ((s32[32,1,2]{2,1,0:T(1,128)}), s32[32,1,2]{2,1,0:T(1,128)S(1)}, u32[]{:S(2)}, u32[]{:S(2)}) async-start(s32[32,1,2]{2,1,0:T(1,128)} %constant_dynamic-slice_fusion), calls=%async_computation | async-start | bytes 32768 | tf_op jit(solution)/shard_map/all_to_all | solution.py:29
  163.0 2.8 all-to-all-done
  165.8 6.0 %all-to-all-start.2 = ((bf16[32,1,2,12288]{3,2,1,0:T(2,128)(2,1)}), bf16[32,1,2,12288]{3,2,1,0:T(2,128)(2,1)S(1)}, u32[]{:S(2)}, u32[]{:S(2)}) async-start(bf16[32,1,2,12288]{3,2,1,0:T(2,128)(2,1)} %reshape.160), calls=%async_computation.2 | async-start | bytes 3145728 | tf_op jit(solution)/shard_map/all_to_all | solution.py:45
  172.5 37.2 %all-to-all-done.2 = bf16[32,1,2,12288]{3,2,1,0:T(2,128)(2,1)S(1)} async-done(((bf16[32,1,2,12288]{3,2,1,0:T(2,128)(2,1)}), bf16[32,1,2,12288]{3,2,1,0:T(2,128)(2,1)S(1)}, u32[]{:S(2)}, u32[]{:S(2)}) %all-to-all-start.2) | async-done | bytes 1572896 | tf_op jit(solution)/shard_map/all_to_all | solution.py:45
  209.6 5.2 %reshape.101 = bf16[64,256,48]{2,1,0:T(8,128)(2,1)} reshape(bf16[32,1,2,12288]{3,2,1,0:T(2,128)(2,1)S(1)} %all-to-all-done.2) | data formatting | bytes 3145728 | tf_op jit(solution)/shard_map/reshape | solution.py:52
  214.8 3.6 fusion.10
  223.3 3.2 copy.72
  226.4 9.3 %reshape.102 = bf16[32,1,2,12288]{3,2,0,1:T(2,128)(2,1)S(1)} reshape(bf16[64,256,48]{2,1,0:T(8,128)(2,1)} %copy.72) | data formatting | bytes 3145728 | tf_op jit(solution)/shard_map/reshape | solution.py:61
  235.7 44.2 %all_to_all.49 = bf16[32,1,2,12288]{3,2,1,0:T(2,128)(2,1)S(1)} all-to-all(bf16[32,1,2,12288]{3,2,1,0:T(2,128)(2,1)S(1)} %bitcast.79), channel_id=1, replica_groups=mesh['member'=8,'space'=32] {'space'}, dimensions={0} | all-to-all | bytes 3145728 | tf_op jit(solution)/shard_map/all_to_all | solution.py:62
  280.0 11.1 %copy.74 = bf16[32,1,2,12288]{0,2,1,3:T(2,128)(2,1)} copy(bf16[32,1,2,12288]{3,2,1,0:T(2,128)(2,1)S(1)} %all_to_all.49) | data formatting | bytes 3145728 | tf_op jit(solution)/shard_map/all_to_all | solution.py:62
  291.1 9.5 %reshape.168 = bf16[8,2,49152]{2,1,0:T(2,128)(2,1)} reshape(bf16[12288,1,2,32]{3,2,1,0:T(2,128)(2,1)} %bitcast.74) | data formatting | bytes 3145728
  300.6 4.8 %all-to-all-start.4 = ((bf16[8,2,49152]{2,1,0:T(2,128)(2,1)}), bf16[8,2,49152]{2,1,0:T(2,128)(2,1)S(1)}, u32[]{:S(2)}, u32[]{:S(2)}) async-start(bf16[8,2,49152]{2,1,0:T(2,128)(2,1)} %reshape.168), calls=%async_computation.4 | async-start | bytes 3145728 | tf_op jit(solution)/shard_map/all_to_all | solution.py:63
  305.4 24.0 %all-to-all-done.4 = bf16[8,2,49152]{2,1,0:T(2,128)(2,1)S(1)} async-done(((bf16[8,2,49152]{2,1,0:T(2,128)(2,1)}), bf16[8,2,49152]{2,1,0:T(2,128)(2,1)S(1)}, u32[]{:S(2)}, u32[]{:S(2)}) %all-to-all-start.4) | async-done | bytes 1572896 | tf_op jit(solution)/shard_map/all_to_all | solution.py:63
  329.4 5.4 %reshape.169 = bf16[12288,1,2,32]{3,2,1,0:T(2,128)(2,1)} reshape(bf16[8,2,49152]{2,1,0:T(2,128)(2,1)S(1)} %all-to-all-done.4) | data formatting | bytes 3145728
  334.9 14.4 %copy.75 = bf16[32,1,2,8,1536]{4,2,3,0,1:T(2,128)(2,1)S(1)} copy(bf16[32,1,2,8,1536]{0,2,4,3,1:T(2,128)(2,1)} %bitcast.75) | data formatting | bytes 3145728 | tf_op jit(solution)/shard_map/all_to_all | solution.py:63
  349.9 2.9 gather_fusion.3
  354.6 2.5 copy.76
  357.0 8.8 %copy.77 = f32[512,32,48]{2,1,0:T(8,128)} copy(f32[512,32,48]{0,2,1:T(8,128)} %bitcast.76) | data formatting | bytes 6291456 | tf_op jit(solution)/shard_map/convert_element_type | solution.py:66
  365.8 6.5 %fusion.2 = bf16[32,48,512]{1,0,2:T(8,128)(2,1)} fusion(f32[512,32,48]{2,1,0:T(8,128)} %copy.77, f32[48,512]{0,1:T(8,128)S(1)} %broadcast_multiply_fusion), kind=kLoop, calls=%fused_computation.10 | loop fusion | flops 1572864 | bytes 4816896 | tf_op jit(solution)/shard_map/convert_element_type | solution.py:66
  372.3 5.4 %copy.78 = bf16[32,48,512]{2,1,0:T(8,128)(2,1)} copy(bf16[32,48,512]{1,0,2:T(8,128)(2,1)} %fusion.2) | data formatting | bytes 3145728
  377.7 2.9 gather_fusion.1
  (53 shorter events, 19.7 us)
Async XLA Ops:
  7.2 16.2 %copy-start = (f32[32,128]{1,0:T(8,128)S(1)}, f32[32,128]{1,0:T(8,128)}, u32[]{:S(2)}) copy-start(f32[32,128]{1,0:T(8,128)} %param.9) | copy-start | bytes 49156
  7.2 103.9 %all-reduce.2.cloned.1.call-start = ((), (), s32[]{:S(2)}) async-start(), calls=%async_computation.5 | async-start | bytes 524288 | tf_op jit(solution)/shard_map/psum | solution.py:32
  14.5 4.8 %copy-start.4 = (s32[512]{0:T(512)S(1)}, s32[512]{0:T(512)}, u32[]{:S(2)}) copy-start(s32[512]{0:T(512)} %param.11) | copy-start | bytes 6148
  130.6 21.1 %all-to-all-start.1 = ((bf16[32,8,2,1536]{3,2,0,1:T(2,128)(2,1)}), bf16[32,8,2,1536]{3,2,0,1:T(2,128)(2,1)S(1)}, u32[]{:S(2)}, u32[]{:S(2)}) async-start(bf16[32,8,2,1536]{3,2,0,1:T(2,128)(2,1)} %copy.65), calls=%async_computation.1 | async-start | bytes 3145728 | tf_op jit(solution)/shard_map/all_to_all | solution.py:46
  151.6 14.2 %all-to-all-start = ((s32[32,1,2]{2,1,0:T(1,128)}), s32[32,1,2]{2,1,0:T(1,128)S(1)}, u32[]{:S(2)}, u32[]{:S(2)}) async-start(s32[32,1,2]{2,1,0:T(1,128)} %constant_dynamic-slice_fusion), calls=%async_computation | async-start | bytes 32768 | tf_op jit(solution)/shard_map/all_to_all | solution.py:29
  165.8 43.8 %all-to-all-start.2 = ((bf16[32,1,2,12288]{3,2,1,0:T(2,128)(2,1)}), bf16[32,1,2,12288]{3,2,1,0:T(2,128)(2,1)S(1)}, u32[]{:S(2)}, u32[]{:S(2)}) async-start(bf16[32,1,2,12288]{3,2,1,0:T(2,128)(2,1)} %reshape.160), calls=%async_computation.2 | async-start | bytes 3145728 | tf_op jit(solution)/shard_map/all_to_all | solution.py:45
  171.8 43.0 %copy-start.3 = (bf16[4,256,256]{2,1,0:T(8,128)(2,1)S(1)}, bf16[4,256,256]{2,1,0:T(8,128)(2,1)}, u32[]{:S(2)}) copy-start(bf16[4,256,256]{2,1,0:T(8,128)(2,1)} %param.10) | copy-start | bytes 1572868
  214.8 3.6 copy-start.2
  300.6 4.8 %copy-start.6 = (s32[128]{0:T(128)S(1)}, s32[128]{0:T(128)}, u32[]{:S(2)}) copy-start(s32[128]{0:T(128)} %param.13) | copy-start | bytes 1540
  300.6 28.8 %all-to-all-start.4 = ((bf16[8,2,49152]{2,1,0:T(2,128)(2,1)}), bf16[8,2,49152]{2,1,0:T(2,128)(2,1)S(1)}, u32[]{:S(2)}, u32[]{:S(2)}) async-start(bf16[8,2,49152]{2,1,0:T(2,128)(2,1)} %reshape.168), calls=%async_computation.4 | async-start | bytes 3145728 | tf_op jit(solution)/shard_map/all_to_all | solution.py:63
  372.3 8.5 %copy-start.5 = (f32[48]{0:T(128)S(1)}, f32[48]{0:T(128)}, u32[]{:S(2)}) copy-start(f32[48]{0:T(128)} %param.12) | copy-start | bytes 580
  372.3 10.1 %copy-start.1 = (f32[32,128]{1,0:T(8,128)S(1)}, f32[32,128]{1,0:T(8,128)}, u32[]{:S(2)}) copy-start(f32[32,128]{1,0:T(8,128)} %param.9) | copy-start | bytes 49156
Sparse Core Ops, SparseCore 0:
  19.4 91.6 all-reduce.1
where the time goes:
time: 391 us; the launch traced here: 389 us
  waiting for transfers between devices  165 us (42%)
  local copies, waits for them, and re-layouts  110 us (28%)
  blocking collectives  44.2 us (11%)
  other arithmetic  23.1 us (6%)
  starting transfers between devices  22.4 us (6%)
  between operations  14.4 us (4%)
  matrix products  10.2 us (3%)
    psum x1, waiting for transfers between devices, local(): summed = lax.psum(jnp.sum(ensemble, axis=0, dtype=jnp.float32), 'member')  83.8 us
    all_to_all x1, blocking collectives, local(): lax.all_to_all(result_rows, 'space', split_axis=0, concat_axis=0, tiled=T...  44.2 us
    all_to_all x1, waiting for transfers between devices, local(): lax.all_to_all(lax.all_to_all(payload, 'member', split_axis=1, concat_axi...  37.2 us
    unnamed x18, local copies, waits for them, and re-layouts  27.6 us
    all_to_all x1, waiting for transfers between devices, local(): lax.all_to_all(halfway, 'member', split_axis=3, concat_axis=1, tiled=True)  24 us
    all_to_all x1, waiting for transfers between devices, local(): lax.all_to_all(payload, 'member', split_axis=1, concat_axis=3, tiled=True)  16.7 us
    all_to_all x1, local copies, waits for them, and re-layouts, local(): lax.all_to_all(halfway, 'member', split_axis=3, concat_axis=1, tiled=True)  14.4 us
    convert_element_type x2, local copies, waits for them, and re-layouts, local(): analysis = (mean[None] + restored.astype(jnp.float32)).astype(jnp.bfloat16)  11.2 us
  transfers between devices with their start and end apart: 5, of which 5 were waited for; matrix products, arithmetic and copies ran while one was open for 3% of the time, Pallas kernels for 0%

commit v1 on v0

--- a/solution.py
+++ b/solution.py
@@ -2,6 +2,12 @@
 import jax.numpy as jnp
 from jax import lax
 from jax.sharding import PartitionSpec as P
+
+
+def add_all(block, axis):
+    parts = lax.all_gather(block, axis, axis=0, tiled=False)
+    result = parts.sum(axis=0)
+    return result
 
 
 def local(ensemble, inflation, weights, region_ids, extinction, obs_cols):
@@ -29,7 +35,7 @@
     got_labels = lax.all_to_all(
         my_labels, "space", split_axis=0, concat_axis=0, tiled=True
     ).reshape(own_cols)
-    summed = lax.psum(jnp.sum(ensemble, axis=0, dtype=jnp.float32), "member")
+    summed = add_all(jnp.sum(ensemble, axis=0, dtype=jnp.float32), "member")
     mean = summed / members
     region_hot = (jnp.arange(all_regions, dtype=jnp.int32)[:, None] == region_ids[None, :]).astype(
         jnp.float32

time: 391 us -> 331 us (0.85)
  waiting for transfers between devices: 165 us -> 78.9 us
  blocking collectives: 44.2 us -> 79.7 us
  between operations: 14.4 us -> 0.98 us
  starting transfers between devices: 22.4 us -> 27.9 us
    psum x1 -> x0, waiting for transfers between devices: 83.8 us -> none  [local(): summed = lax.psum(jnp.sum(ensemble, axis=0, dtype=jnp.float32), 'member')]
    all_gather x0 -> x1, blocking collectives: none -> 35.4 us  [add_all(): parts = lax.all_gather(block, axis, axis=0, tiled=False)]
    unnamed x18 -> x20, local copies, waits for them, and re-layouts: 27.6 us -> 26.9 us
  transfers between devices with their start and end apart: 5 -> 4, of which waited for: 5 -> 4; matrix products, arithmetic and copies ran while one was open for 3% -> 1% of each run, Pallas kernels for 0% -> 0%
where the time goes in v1:
time: 331 us; the launch traced here: 330 us
  local copies, waits for them, and re-layouts  110 us (33%)
  blocking collectives  79.7 us (24%)
  waiting for transfers between devices  78.9 us (24%)
  starting transfers between devices  27.9 us (8%)
  other arithmetic  22.3 us (7%)
  matrix products  10.2 us (3%)
    all_to_all x1, blocking collectives, local(): lax.all_to_all(result_rows, 'space', split_axis=0, concat_axis=0, tiled=T...  44.2 us
    all_to_all x1, waiting for transfers between devices, local(): lax.all_to_all(lax.all_to_all(payload, 'member', split_axis=1, concat_axi...  37.2 us
    all_gather x1, blocking collectives, add_all(): parts = lax.all_gather(block, axis, axis=0, tiled=False)  35.4 us
    unnamed x20, local copies, waits for them, and re-layouts  26.9 us
    all_to_all x1, waiting for transfers between devices, local(): lax.all_to_all(halfway, 'member', split_axis=3, concat_axis=1, tiled=True)  24 us
    all_to_all x1, waiting for transfers between devices, local(): lax.all_to_all(payload, 'member', split_axis=1, concat_axis=3, tiled=True)  14.9 us
    all_to_all x1, local copies, waits for them, and re-layouts, local(): lax.all_to_all(halfway, 'member', split_axis=3, concat_axis=1, tiled=True)  14.4 us
    convert_element_type x2, local copies, waits for them, and re-layouts, local(): analysis = (mean[None] + restored.astype(jnp.float32)).astype(jnp.bfloat16)  11.2 us
  transfers between devices with their start and end apart: 4, of which 4 were waited for; matrix products, arithmetic and copies ran while one was open for 1% of the time, Pallas kernels for 0%

profile of v1, /device:TPU:64, one launch (start us, length us, event | category | flops | bytes accessed | tf_op | source)
XLA Modules:
  0.0 329.9 jit_solution(7407053213847845103)
XLA Ops:
  3.0 2.4 scatter_custom_fusion
  5.5 3.5 %gather_fusion = s32[512]{0:T(512)S(1)} fusion(s32[512]{0:T(512)S(1)} %get-tuple-element.21, s32[1024]{0:T(1024)S(1)} %pad_clamp_fusion.2), kind=kCustom, calls=%fused_computation.2 | custom fusion | bytes 6144 | tf_op jit(solution)/shard_map/jit(_take)/gather | solution.py:33
  9.0 6.5 %copy.61 = bf16[32,48,512]{1,0,2:T(8,128)(2,1)} copy(bf16[32,48,512]{2,1,0:T(8,128)(2,1)S(1)} %copy-done.3) | data formatting | bytes 3145728 | tf_op args[0]
  15.6 4.1 %convert_reduce_fusion = f32[48,512]{0,1:T(8,128)S(1)} fusion(bf16[32,48,512]{1,0,2:T(8,128)(2,1)} %copy.61), kind=kLoop, calls=%fused_computation.6 | loop fusion | flops 1548288 | bytes 1671168 | tf_op jit(solution)/shard_map/reduce_sum | solution.py:38
  19.7 35.4 %all-gather = f32[384,512]{1,0:T(8,128)S(1)} all-gather(f32[48,512]{1,0:T(8,128)S(1)} %copy.62), channel_id=2, replica_groups=mesh['member'=8,'space'=32] {'member'}, dimensions={0}, use_global_device_ids=true | all-gather | bytes 884736 | tf_op jit(solution)/shard_map/all_gather | solution.py:8
  55.8 5.8 %fusion.3 = bf16[512,32,48]{2,1,0:T(8,128)(2,1)} fusion(bf16[32,48,512]{1,0,2:T(8,128)(2,1)} %copy.61, f32[32,512]{0,1:T(8,128)S(1)} %copy.65, f32[48,512]{0,1:T(8,128)S(1)} %copy.63), kind=kLoop, calls=%fused_computation.11 | loop fusion | flops 3145728 | bytes 3309568 | tf_op jit(solution)/shard_map/transpose | solution.py:47
  61.6 4.4 %copy.66 = bf16[512,32,48]{0,2,1:T(8,128)(2,1)S(1)} copy(bf16[512,32,48]{2,1,0:T(8,128)(2,1)} %fusion.3) | data formatting | bytes 3145728 | tf_op jit(solution)/shard_map/transpose | solution.py:47
  66.7 2.9 gather_fusion.2
  71.9 2.4 copy.68
  74.3 7.0 %all-to-all-start.1 = ((bf16[32,8,2,1536]{3,2,0,1:T(2,128)(2,1)}), bf16[32,8,2,1536]{3,2,0,1:T(2,128)(2,1)S(1)}, u32[]{:S(2)}, u32[]{:S(2)}) async-start(bf16[32,8,2,1536]{3,2,0,1:T(2,128)(2,1)} %copy.68), calls=%async_computation.1 | async-start | bytes 3145728 | tf_op jit(solution)/shard_map/all_to_all | solution.py:52
  82.0 14.9 %all-to-all-done.1 = bf16[32,8,2,1536]{3,2,0,1:T(2,128)(2,1)S(1)} async-done(((bf16[32,8,2,1536]{3,2,0,1:T(2,128)(2,1)}), bf16[32,8,2,1536]{3,2,0,1:T(2,128)(2,1)S(1)}, u32[]{:S(2)}, u32[]{:S(2)}) %all-to-all-start.1) | async-done | bytes 1572896 | tf_op jit(solution)/shard_map/all_to_all | solution.py:52
  96.9 8.8 %all-to-all-start = ((s32[32,1,2]{2,1,0:T(1,128)}), s32[32,1,2]{2,1,0:T(1,128)S(1)}, u32[]{:S(2)}, u32[]{:S(2)}) async-start(s32[32,1,2]{2,1,0:T(1,128)} %constant_dynamic-slice_fusion), calls=%async_computation | async-start | bytes 32768 | tf_op jit(solution)/shard_map/all_to_all | solution.py:35
  109.1 2.8 all-to-all-done
  112.0 6.0 %all-to-all-start.2 = ((bf16[32,1,2,12288]{3,2,1,0:T(2,128)(2,1)}), bf16[32,1,2,12288]{3,2,1,0:T(2,128)(2,1)S(1)}, u32[]{:S(2)}, u32[]{:S(2)}) async-start(bf16[32,1,2,12288]{3,2,1,0:T(2,128)(2,1)} %reshape.163), calls=%async_computation.2 | async-start | bytes 3145728 | tf_op jit(solution)/shard_map/all_to_all | solution.py:51
  118.7 37.2 %all-to-all-done.2 = bf16[32,1,2,12288]{3,2,1,0:T(2,128)(2,1)S(1)} async-done(((bf16[32,1,2,12288]{3,2,1,0:T(2,128)(2,1)}), bf16[32,1,2,12288]{3,2,1,0:T(2,128)(2,1)S(1)}, u32[]{:S(2)}, u32[]{:S(2)}) %all-to-all-start.2) | async-done | bytes 1572896 | tf_op jit(solution)/shard_map/all_to_all | solution.py:51
  155.8 5.2 %reshape.103 = bf16[64,256,48]{2,1,0:T(8,128)(2,1)} reshape(bf16[32,1,2,12288]{3,2,1,0:T(2,128)(2,1)S(1)} %all-to-all-done.2) | data formatting | bytes 3145728 | tf_op jit(solution)/shard_map/reshape | solution.py:58
  161.0 3.6 %fusion.10 = f32[64,48,256]{2,1,0:T(8,128)S(1)} fusion(bf16[64,256,48]{2,1,0:T(8,128)(2,1)} %reshape.103, bf16[4,256,256]{2,1,0:T(8,128)(2,1)S(1)} %copy-done.4), kind=kOutput, calls=%fused_computation.24 | convolution fusion | flops 402653184 | bytes 4849664 | tf_op jit(solution)/shard_map/jk,cjt->ckt/dot_general | solution.py:61
  169.5 3.2 copy.75
  172.6 9.3 %reshape.104 = bf16[32,1,2,12288]{3,2,0,1:T(2,128)(2,1)S(1)} reshape(bf16[64,256,48]{2,1,0:T(8,128)(2,1)} %copy.75) | data formatting | bytes 3145728 | tf_op jit(solution)/shard_map/reshape | solution.py:67
  181.9 44.2 %all_to_all.49 = bf16[32,1,2,12288]{3,2,1,0:T(2,128)(2,1)S(1)} all-to-all(bf16[32,1,2,12288]{3,2,1,0:T(2,128)(2,1)S(1)} %bitcast.80), channel_id=1, replica_groups=mesh['member'=8,'space'=32] {'space'}, dimensions={0} | all-to-all | bytes 3145728 | tf_op jit(solution)/shard_map/all_to_all | solution.py:68
  226.1 11.1 %copy.77 = bf16[32,1,2,12288]{0,2,1,3:T(2,128)(2,1)} copy(bf16[32,1,2,12288]{3,2,1,0:T(2,128)(2,1)S(1)} %all_to_all.49) | data formatting | bytes 3145728 | tf_op jit(solution)/shard_map/all_to_all | solution.py:68
  237.2 9.5 %reshape.171 = bf16[8,2,49152]{2,1,0:T(2,128)(2,1)} reshape(bf16[12288,1,2,32]{3,2,1,0:T(2,128)(2,1)} %bitcast.75) | data formatting | bytes 3145728
  246.7 6.1 %all-to-all-start.4 = ((bf16[8,2,49152]{2,1,0:T(2,128)(2,1)}), bf16[8,2,49152]{2,1,0:T(2,128)(2,1)S(1)}, u32[]{:S(2)}, u32[]{:S(2)}) async-start(bf16[8,2,49152]{2,1,0:T(2,128)(2,1)} %reshape.171), calls=%async_computation.4 | async-start | bytes 3145728 | tf_op jit(solution)/shard_map/all_to_all | solution.py:69
  252.9 24.0 %all-to-all-done.4 = bf16[8,2,49152]{2,1,0:T(2,128)(2,1)S(1)} async-done(((bf16[8,2,49152]{2,1,0:T(2,128)(2,1)}), bf16[8,2,49152]{2,1,0:T(2,128)(2,1)S(1)}, u32[]{:S(2)}, u32[]{:S(2)}) %all-to-all-start.4) | async-done | bytes 1572896 | tf_op jit(solution)/shard_map/all_to_all | solution.py:69
  276.9 5.4 %reshape.172 = bf16[12288,1,2,32]{3,2,1,0:T(2,128)(2,1)} reshape(bf16[8,2,49152]{2,1,0:T(2,128)(2,1)S(1)} %all-to-all-done.4) | data formatting | bytes 3145728
  282.3 14.4 %copy.78 = bf16[32,1,2,8,1536]{4,2,3,0,1:T(2,128)(2,1)S(1)} copy(bf16[32,1,2,8,1536]{0,2,4,3,1:T(2,128)(2,1)} %bitcast.76) | data formatting | bytes 3145728 | tf_op jit(solution)/shard_map/all_to_all | solution.py:69
  297.4 2.9 gather_fusion.3
  302.0 2.5 copy.79
  304.5 8.8 %copy.80 = f32[512,32,48]{2,1,0:T(8,128)} copy(f32[512,32,48]{0,2,1:T(8,128)} %bitcast.77) | data formatting | bytes 6291456 | tf_op jit(solution)/shard_map/convert_element_type | solution.py:72
  313.2 6.5 %fusion.2 = bf16[32,48,512]{1,0,2:T(8,128)(2,1)} fusion(f32[512,32,48]{2,1,0:T(8,128)} %copy.80, f32[48,512]{0,1:T(8,128)S(1)} %copy.63), kind=kLoop, calls=%fused_computation.10 | loop fusion | flops 1572864 | bytes 4816896 | tf_op jit(solution)/shard_map/convert_element_type | solution.py:72
  319.8 5.4 %copy.81 = bf16[32,48,512]{2,1,0:T(8,128)(2,1)} copy(bf16[32,48,512]{1,0,2:T(8,128)(2,1)} %fusion.2) | data formatting | bytes 3145728
  325.1 2.9 gather_fusion.1
  (56 shorter events, 19.7 us)
Async XLA Ops:
  0.6 54.8 %copy-start = (f32[32,128]{1,0:T(8,128)S(1)}, f32[32,128]{1,0:T(8,128)}, u32[]{:S(2)}) copy-start(f32[32,128]{1,0:T(8,128)} %param.9) | copy-start | bytes 49156
  0.6 8.4 %copy-start.3 = (bf16[32,48,512]{2,1,0:T(8,128)(2,1)S(1)}, bf16[32,48,512]{2,1,0:T(8,128)(2,1)}, u32[]{:S(2)}) copy-start(bf16[32,48,512]{2,1,0:T(8,128)(2,1)} %param.8) | copy-start | bytes 4718596
  15.6 39.8 %copy-start.5 = (s32[512]{0:T(512)S(1)}, s32[512]{0:T(512)}, u32[]{:S(2)}) copy-start(s32[512]{0:T(512)} %param.11) | copy-start | bytes 6148
  74.3 22.6 %all-to-all-start.1 = ((bf16[32,8,2,1536]{3,2,0,1:T(2,128)(2,1)}), bf16[32,8,2,1536]{3,2,0,1:T(2,128)(2,1)S(1)}, u32[]{:S(2)}, u32[]{:S(2)}) async-start(bf16[32,8,2,1536]{3,2,0,1:T(2,128)(2,1)} %copy.68), calls=%async_computation.1 | async-start | bytes 3145728 | tf_op jit(solution)/shard_map/all_to_all | solution.py:52
  96.9 15.0 %all-to-all-start = ((s32[32,1,2]{2,1,0:T(1,128)}), s32[32,1,2]{2,1,0:T(1,128)S(1)}, u32[]{:S(2)}, u32[]{:S(2)}) async-start(s32[32,1,2]{2,1,0:T(1,128)} %constant_dynamic-slice_fusion), calls=%async_computation | async-start | bytes 32768 | tf_op jit(solution)/shard_map/all_to_all | solution.py:35
  112.0 43.8 %all-to-all-start.2 = ((bf16[32,1,2,12288]{3,2,1,0:T(2,128)(2,1)}), bf16[32,1,2,12288]{3,2,1,0:T(2,128)(2,1)S(1)}, u32[]{:S(2)}, u32[]{:S(2)}) async-start(bf16[32,1,2,12288]{3,2,1,0:T(2,128)(2,1)} %reshape.163), calls=%async_computation.2 | async-start | bytes 3145728 | tf_op jit(solution)/shard_map/all_to_all | solution.py:51
  118.0 43.0 %copy-start.4 = (bf16[4,256,256]{2,1,0:T(8,128)(2,1)S(1)}, bf16[4,256,256]{2,1,0:T(8,128)(2,1)}, u32[]{:S(2)}) copy-start(bf16[4,256,256]{2,1,0:T(8,128)(2,1)} %param.10) | copy-start | bytes 1572868
  161.0 3.6 %copy-start.2 = (bf16[64,256,48]{2,1,0:T(8,128)(2,1)S(1)}, bf16[64,256,48]{2,1,0:T(8,128)(2,1)}, u32[]{:S(2)}) copy-start(bf16[64,256,48]{2,1,0:T(8,128)(2,1)} %reshape.103) | copy-start | bytes 4718596
  246.7 6.1 %copy-start.7 = (s32[128]{0:T(128)S(1)}, s32[128]{0:T(128)}, u32[]{:S(2)}) copy-start(s32[128]{0:T(128)} %param.13) | copy-start | bytes 1540
  246.7 30.1 %all-to-all-start.4 = ((bf16[8,2,49152]{2,1,0:T(2,128)(2,1)}), bf16[8,2,49152]{2,1,0:T(2,128)(2,1)S(1)}, u32[]{:S(2)}, u32[]{:S(2)}) async-start(bf16[8,2,49152]{2,1,0:T(2,128)(2,1)} %reshape.171), calls=%async_computation.4 | async-start | bytes 3145728 | tf_op jit(solution)/shard_map/all_to_all | solution.py:69
  319.8 8.5 %copy-start.6 = (f32[48]{0:T(128)S(1)}, f32[48]{0:T(128)}, u32[]{:S(2)}) copy-start(f32[48]{0:T(128)} %param.12) | copy-start | bytes 580
  319.8 10.1 %copy-start.1 = (f32[32,128]{1,0:T(8,128)S(1)}, f32[32,128]{1,0:T(8,128)}, u32[]{:S(2)}) copy-start(f32[32,128]{1,0:T(8,128)} %param.9) | copy-start | bytes 49156
